TPU v7x, 32 devices: a whole 2x2x4 slice. The times are simulated.
32 devices in a mesh: section: 2 (over core), dp: 16 (over z, y, x).
Axes of the slice: x: 2, y: 2, z: 4, core: 2. Of those that a mesh axis runs over, the one named last changes fastest.
Arguments:
- acts: bfloat16 [2, 16, 1, 64, 2, 2, 128], P('section', 'dp'), may hold values from -6 to 6
- preacts: bfloat16 [2, 16, 1, 64, 2, 2, 128], P('section', 'dp'), may hold values from -6 to 6
- top_grad: bfloat16 [16, 1, 64, 2, 2, 128], P('dp'), may hold values from -6 to 6
- weights: bfloat16 [2, 64, 1728], P('section'), may hold values from -0.21875 to 0.21875
- a_factor: bfloat16 [2, 1728, 1728], P('section', 'dp'), as said below
- g_factor: bfloat16 [2, 64, 64], P('section'), as said below
Outputs:
- act_grads: bfloat16 [2, 16, 1, 64, 2, 2, 128], P('section', 'dp')
- update: float32 [2, 1728, 64], P('section', 'dp')
- inverse: float32 [2, 1728, 1728], P('section', 'dp')
Inputs may be any that keep to these rules, and one draw needn't show every extreme that they name: `a_factor`: each matrix is symmetric and positive definite. `g_factor`: each matrix is symmetric and positive definite.
All inputs are finite; a program needn't handle non-finite values. Where the computation divides by a largest or mean magnitude, that divisor is 1e-20 or more.
Results may differ from a plain program's by a relative error of at most 0.006.
Values may be sent and summed in bfloat16 or wider, within the bound.
No kernel may reach another device: no remote copies, remote signals or barrier semaphores. Data moves between devices by JAX's collectives and lax.ppermute only.
A program may use at most 64 MiB of HBM per device.

v0:
```python
import jax
import jax.numpy as jnp
from jax import lax
from jax.sharding import PartitionSpec as P

KW = 3
MICRO = 1


def shifted(value, axis, steps):
    count = lax.axis_size(axis)
    first, last = (max(0, -steps), min(count, count - steps))
    return lax.ppermute(value, axis, [(source, source + steps) for source in range(first, last)])


def tap_offsets(kernel_width):
    middle = kernel_width // 2
    result = []
    for along_x in range(kernel_width):
        for along_y in range(kernel_width):
            for along_z in range(kernel_width):
                result.append((along_x - middle, along_y - middle, along_z - middle))
    return result


def taps_stack(volume, kernel_width, direction):
    middle = kernel_width // 2
    padded = jnp.pad(volume, ((0, 0), (middle, middle), (middle, middle), (middle, middle)))
    size_x, size_y, size_z = (volume.shape[1], volume.shape[2], volume.shape[3])
    pieces = []
    for off_x, off_y, off_z in tap_offsets(kernel_width):
        start_x = middle + direction * off_x
        start_y = middle + direction * off_y
        start_z = middle + direction * off_z
        pieces.append(
            padded[
                :,
                start_x : start_x + size_x,
                start_y : start_y + size_y,
                start_z : start_z + size_z,
            ]
        )
    stacked = jnp.stack(pieces, 0)
    return stacked.reshape(len(pieces) * volume.shape[0], size_x * size_y * size_z)


def back_input(grad_out, w_rows):
    columns = taps_stack(grad_out, KW, -1)
    summed = lax.dot_general(
        w_rows, columns, (((0,), (0,)), ((), ())), preferred_element_type=jnp.float32
    )
    return summed.astype(jnp.bfloat16).reshape(grad_out.shape)


def back_weight(volume, grad_out):
    columns = taps_stack(volume, KW, 1)
    flattened = grad_out.reshape(grad_out.shape[0], -1)
    return lax.dot_general(
        columns, flattened, (((1,), (1,)), ((), ())), preferred_element_type=jnp.float32
    )


def local_inverse(matrix):
    values = matrix.astype(jnp.float32)
    step_size = 1.0 / jnp.max(jnp.sum(jnp.abs(values), axis=1))
    identity = jnp.eye(matrix.shape[0], dtype=jnp.float32)
    resid0 = (identity - step_size * values).astype(jnp.bfloat16)
    resid1 = jnp.dot(resid0, resid0, preferred_element_type=jnp.float32).astype(jnp.bfloat16)
    cross_term = jnp.dot(resid1, resid0, preferred_element_type=jnp.float32)
    return step_size * (
        identity + resid0.astype(jnp.float32) + resid1.astype(jnp.float32) + cross_term
    )


def eye_rows(start_row, row_total, order_full):
    column_ids = lax.broadcasted_iota(jnp.int32, (row_total, order_full), 1)
    row_ids = lax.broadcasted_iota(jnp.int32, (row_total, order_full), 0)
    return (column_ids == start_row + row_ids).astype(jnp.float32)


def shards(acts, preacts, top_grad, weights, a_factor, g_factor):
    section_index = lax.axis_index("section")
    section_count = lax.axis_size("section")
    tick_count = MICRO + section_count - 1
    inputs = acts[0, 0]
    pre_values = preacts[0, 0]
    upper_grads = top_grad[0]
    channels = weights.shape[1]
    w_rows = weights[0].reshape(channels, -1, channels).transpose(1, 0, 2).reshape(-1, channels)
    zero_field = jnp.zeros(inputs.shape[1:], jnp.bfloat16)

    def one_tick(tick_index, carried):
        outgoing, stored_grads, stored_slopes = carried
        incoming = shifted(outgoing, "section", -1)
        micro_index = tick_index - (section_count - 1 - section_index)
        is_valid = jnp.logical_and(micro_index >= 0, micro_index < MICRO)
        clipped = jnp.clip(micro_index, 0, MICRO - 1)
        from_top = lax.dynamic_index_in_dim(upper_grads, clipped, 0, keepdims=False)
        arriving = jnp.where(section_index == section_count - 1, from_top, incoming)
        pre_now = lax.dynamic_index_in_dim(pre_values, clipped, 0, keepdims=False)
        grad_out = jnp.where(pre_now > 0, arriving, zero_field)
        sending = back_input(grad_out, w_rows)
        old_grad = lax.dynamic_index_in_dim(stored_grads, clipped, 0, keepdims=False)
        old_slope = lax.dynamic_index_in_dim(stored_slopes, clipped, 0, keepdims=False)
        stored_grads = lax.dynamic_update_index_in_dim(
            stored_grads, jnp.where(is_valid, sending, old_grad), clipped, 0
        )
        stored_slopes = lax.dynamic_update_index_in_dim(
            stored_slopes, jnp.where(is_valid, grad_out, old_slope), clipped, 0
        )
        return (sending, stored_grads, stored_slopes)

    start_state = (
        zero_field,
        jnp.zeros(inputs.shape, jnp.bfloat16),
        jnp.zeros(inputs.shape, jnp.bfloat16),
    )
    last_sent, stored_grads, stored_slopes = lax.fori_loop(0, tick_count, one_tick, start_state)
    local_grad = back_weight(inputs[0], stored_slopes[0])
    summed_grad = lax.psum(local_grad, "dp")
    mean_grad = summed_grad / lax.axis_size("dp")
    a_rows = a_factor[0]
    row_total = a_rows.shape[0]
    order_full = a_rows.shape[1]
    first_row = lax.axis_index("dp") * row_total
    local_max = jnp.max(jnp.sum(jnp.abs(a_rows.astype(jnp.float32)), axis=1))
    step_size = 1.0 / lax.pmax(local_max, "dp")
    own_eye = eye_rows(first_row, row_total, order_full)
    resid0 = (own_eye - step_size * a_rows.astype(jnp.float32)).astype(jnp.bfloat16)
    left_cols = resid0
    resid1 = jnp.dot(
        left_cols,
        lax.all_gather(resid0, "dp", axis=0, tiled=True),
        preferred_element_type=jnp.float32,
    ).astype(jnp.bfloat16)
    left_cols = resid1
    cross_term = jnp.dot(
        left_cols,
        lax.all_gather(resid0, "dp", axis=0, tiled=True),
        preferred_element_type=jnp.float32,
    )
    inverse_rows = step_size * (
        own_eye + resid0.astype(jnp.float32) + resid1.astype(jnp.float32) + cross_term
    )
    g_inverse = local_inverse(g_factor[0])
    preconditioned = jnp.dot(
        mean_grad, g_inverse, precision=lax.Precision.HIGHEST, preferred_element_type=jnp.float32
    )
    update_rows = jnp.dot(
        inverse_rows,
        preconditioned,
        precision=lax.Precision.HIGHEST,
        preferred_element_type=jnp.float32,
    )
    return (stored_grads[None, None], update_rows[None], inverse_rows[None])


def solution(mesh):
    placed = (
        P("section", "dp", None, None, None, None, None),
        P("section", "dp", None, None, None, None, None),
        P("dp", None, None, None, None, None),
        P("section", None, None),
        P("section", "dp", None),
        P("section", None, None),
    )
    return jax.shard_map(
        shards,
        mesh=mesh,
        in_specs=placed,
        out_specs=(
            P("section", "dp", None, None, None, None, None),
            P("section", "dp", None),
            P("section", "dp", None),
        ),
        check_vma=False,
    )
```

profile of v0, /device:TPU:0, one launch (start us, length us, event | category | flops | bytes accessed | tf_op | source)
XLA Modules:
  0.0 278.0 jit_solution(16409648565365553291)
XLA Ops:
  7.2 1.5 reshape_squeeze.6
  8.7 0.9 copy.18
  13.2 2.1 reshape.70
  15.3 0.7 broadcast.39
  16.0 0.7 broadcast.40
  16.6 24.1 %while.20 = (s32[]{:T(128)}, bf16[64,2,2,128]{3,2,1,0:T(2,128)(2,1)}, bf16[1,64,2,2,128]{4,3,2,1,0:T(2,128)(2,1)}, bf16[1,64,2,2,128]{4,3,2,1,0:T(2,128)(2,1)}, ...) while((s32[]{:T(128)}, ...), condition=%wide.region_1.2_spmd.clone, body=%wide.region_0.1_spmd.clone.sunk | while | flops 113475592 | bytes 10772739 | solution.py:118
  16.6 1.3 collective-permute-start
  17.9 2.0 collective-permute-done
  20.0 1.7 fusion.173
  25.0 0.7 reshape.79
  25.7 1.5 fusion.200
  27.2 0.6 reshape.80
  28.0 0.6 copy-done.5
  28.6 1.3 collective-permute-start
  29.9 2.0 collective-permute-done
  32.0 1.7 fusion.173
  37.0 0.7 reshape.79
  37.8 1.5 fusion.200
  39.3 0.6 reshape.80
  40.1 0.6 copy-done.5
  40.7 0.9 reshape_squeeze.7
  42.2 2.9 %fusion.129 = f32[1728,64]{0,1:T(8,128)} fusion(bf16[1728,512]{1,0:T(8,128)(2,1)} %reshape.70, bf16[64,512]{1,0:T(8,128)(2,1)S(1)} %reshape_squeeze.7), kind=kOutput, calls=%fused_computation.203 | convolution fusion | flops 113246208 | bytes 2277376 | tf_op jit(solution)/shard_map/dot_general | solution.py:58
  45.2 44.4 %pmax.7 = f32[]{:T(128)} all-reduce(f32[]{:T(128)} %reduce_max.18), channel_id=1, replica_groups=mesh['section'=2,'dp'=16] {'dp'}, use_global_device_ids=true, to_apply=%region_4.5 | all-reduce | flops 1 | bytes 8 | tf_op jit(solution)/shard_map/pmax | solution.py:127
  90.3 1.0 fusion.128
  93.0 64.2 %all-reduce.4.cloned.1.call-done = f32[1728,64]{0,1:T(8,128)} async-done(((f32[1728,64]{0,1:T(8,128)}), f32[1728,64]{0,1:T(8,128)}) %all-reduce.4.cloned.1.call-update) | async-done | bytes 442384 | tf_op jit(solution)/shard_map/psum | solution.py:120
  157.1 1.6 fusion.60
  158.7 94.8 %all-gather.3.cloned.1.call-done = bf16[16,108,1728]{2,1,0:T(8,128)(2,1)} async-done(((bf16[1,108,1728]{2,1,0:T(8,128)(2,1)}), bf16[16,108,1728]{2,1,0:T(8,128)(2,1)}) %all-gather.3.cloned.1.call-update) | async-done | bytes 5971984 | tf_op jit(solution)/shard_map/all_gather | solution.py:133
  253.5 8.7 %reshape.72 = bf16[1728,1728]{1,0:T(8,128)(2,1)} reshape(bf16[16,108,1728]{2,1,0:T(8,128)(2,1)} %all-gather.3.cloned.1.call-done) | data formatting | bytes 11943936
  262.3 4.0 %convolution_convert_fusion.1 = bf16[108,1728]{1,0:T(8,128)(2,1)S(1)} fusion(bf16[1728,1728]{1,0:T(8,128)(2,1)} %reshape.72, bf16[1,108,1728]{2,1,0:T(8,128)(2,1)S(1)} %copy-done.3, f32[]{:T(128)S(6)} %div.12, s32[108]{0:T(128)S(1)} %iota_add_fusion), kind=kOutput, calls=%fused_computation.115 | convolution fusion | flops 646278912 | bytes 6718900 | tf_op jit(solution)/shard_map/dot_general | solution.py:131
  266.8 1.1 fusion.54
  267.9 1.6 convolution_bitcast_fusion
  269.5 1.7 copy.17
  (113 shorter events, 12.8 us)
Async XLA Ops:
  7.2 2.5 copy-start.2
  7.2 2.6 copy-start.1
  7.2 149.9 %all-reduce.4.cloned.1.call-start = ((), (), s32[]{:S(2)}) async-start(), calls=%async_computation | async-start | bytes 917504 | tf_op jit(solution)/shard_map/psum | solution.py:120
  16.6 3.3 %collective-permute-start = (bf16[64,2,2,128]{3,2,1,0:T(2,128)(2,1)}, bf16[64,2,2,128]{3,2,1,0:T(2,128)(2,1)S(1)}, u32[]{:S(2)}, u32[]{:S(2)}) collective-permute-start(bf16[64,2,2,128]{3,2,1,0:T(2,128)(2,1)} %get-tuple-element.362), channel_id=1, source_target_pairs={{16,0},{17,1},{18,2},{19,3},{20,4},{21,5},{22,6},{23,7},{24,8},{25... | collective-permute-start | bytes 196616 | tf_op jit(solution)/shard_map/while/body/eval_jaxpr/ppermute | solution.py:13
  25.7 2.2 copy-start.4
  28.0 0.6 copy-start.5
  28.6 3.3 %collective-permute-start = (bf16[64,2,2,128]{3,2,1,0:T(2,128)(2,1)}, bf16[64,2,2,128]{3,2,1,0:T(2,128)(2,1)S(1)}, u32[]{:S(2)}, u32[]{:S(2)}) collective-permute-start(bf16[64,2,2,128]{3,2,1,0:T(2,128)(2,1)} %get-tuple-element.362), channel_id=1, source_target_pairs={{16,0},{17,1},{18,2},{19,3},{20,4},{21,5},{22,6},{23,7},{24,8},{25... | collective-permute-start | bytes 196616 | tf_op jit(solution)/shard_map/while/body/eval_jaxpr/ppermute | solution.py:13
  37.8 2.2 copy-start.4
  40.1 0.6 copy-start.5
  40.7 49.6 %copy-start.3 = (bf16[1,108,1728]{2,1,0:T(8,128)(2,1)S(1)}, bf16[1,108,1728]{2,1,0:T(8,128)(2,1)}, u32[]{:S(2)}) copy-start(bf16[1,108,1728]{2,1,0:T(8,128)(2,1)} %param.12) | copy-start | bytes 1119748
  42.2 49.1 %copy-start.6 = (bf16[1,64,64]{2,1,0:T(8,128)(2,1)S(1)}, bf16[1,64,64]{2,1,0:T(8,128)(2,1)}, u32[]{:S(2)}) copy-start(bf16[1,64,64]{2,1,0:T(8,128)(2,1)} %param.13) | copy-start | bytes 24580
  45.1 208.4 %all-gather.3.cloned.1.call-start = ((), (), s32[]{:S(2)}) async-start(), calls=%async_computation.1 | async-start | bytes 6823936 | tf_op jit(solution)/shard_map/all_gather | solution.py:133
  262.3 4.5 %copy-start = (bf16[1728,1728]{1,0:T(8,128)(2,1)S(1)}, bf16[1728,1728]{1,0:T(8,128)(2,1)}, u32[]{:S(2)}) copy-start(bf16[1728,1728]{1,0:T(8,128)(2,1)} %reshape.72) | copy-start | bytes 17915908
Sparse Core Ops, SparseCore 0:
  45.3 111.8 all-reduce.3
  159.9 93.6 all-gather.2
where the time goes:
time: 279 us; the launch traced here: 278 us
  waiting for transfers between devices  163 us (58%)
  blocking collectives  44.4 us (16%)
  local copies, waits for them, and re-layouts  31.8 us (11%)
  between operations  15.5 us (6%)
  matrix products  14.4 us (5%)
  other arithmetic  6.04 us (2%)
    all_gather x1, waiting for transfers between devices, shards(): lax.all_gather(resid0, 'dp', axis=0, tiled=True)  94.8 us
    psum x1, waiting for transfers between devices, shards(): summed_grad = lax.psum(local_grad, 'dp')  64.2 us
    pmax x1, blocking collectives, shards(): step_size = 1.0 / lax.pmax(local_max, 'dp')  44.4 us
    unnamed x39, local copies, waits for them, and re-layouts  15.1 us
    while x60, local copies, waits for them, and re-layouts  7.65 us
  transfers between devices with their start and end apart: 4, of which 4 were waited for; matrix products, arithmetic and copies ran while one was open for 1% of the time, Pallas kernels for 0%

commit v1 on v0

--- a/solution.py
+++ b/solution.py
@@ -2,6 +2,7 @@
 import jax.numpy as jnp
 from jax import lax
 from jax.sharding import PartitionSpec as P
+from jax.lax import ppermute, psum
 
 KW = 3
 MICRO = 1
@@ -117,7 +118,20 @@
     )
     last_sent, stored_grads, stored_slopes = lax.fori_loop(0, tick_count, one_tick, start_state)
     local_grad = back_weight(inputs[0], stored_slopes[0])
-    summed_grad = lax.psum(local_grad, "dp")
+
+    def column_test(inner_x):
+        net_axis = "dp"
+        even = inner_x
+        dev_count = psum(1, axis_name=net_axis)
+        for pp in [
+            [(to_i, to_i ^ k0) for to_i in range(dev_count)]
+            for k0 in (1, 2, 4, 8, 16)
+            if k0 < dev_count
+        ]:
+            even = even + ppermute(even, net_axis, pp)
+        return even
+
+    summed_grad = column_test(local_grad)
     mean_grad = summed_grad / lax.axis_size("dp")
     a_rows = a_factor[0]
     row_total = a_rows.shape[0]

time: 279 us -> 205 us (0.73)
  waiting for transfers between devices: 163 us -> 85.5 us
  starting transfers between devices: 2.64 us -> 9.19 us
  local copies, waits for them, and re-layouts: 31.8 us -> 28.9 us
    all_gather x1, waiting for transfers between devices: 94.8 us -> 0.02 us  [shards(): lax.all_gather(resid0, 'dp', axis=0, tiled=True)]
    ppermute x0 -> x4, waiting for transfers between devices: none -> 81.7 us  [column_test(): even = even + ppermute(even, net_axis, pp)]
    psum x1 -> x0, waiting for transfers between devices: 64.2 us -> none  [shards(): summed_grad = lax.psum(local_grad, 'dp')]
    ppermute x0 -> x4, starting transfers between devices: none -> 6.59 us  [column_test(): even = even + ppermute(even, net_axis, pp)]
  transfers between devices with their start and end apart: 4 -> 7, of which waited for: 4 -> 6; matrix products, arithmetic and copies ran while one was open for 1% -> 13% of each run, Pallas kernels for 0% -> 0%
where the time goes in v1:
time: 205 us; the launch traced here: 204 us
  waiting for transfers between devices  85.5 us (42%)
  blocking collectives  44.1 us (22%)
  local copies, waits for them, and re-layouts  28.9 us (14%)
  between operations  15.6 us (8%)
  matrix products  12.6 us (6%)
  starting transfers between devices  9.19 us (4%)
  other arithmetic  8.32 us (4%)
    ppermute x4, waiting for transfers between devices, column_test(): even = even + ppermute(even, net_axis, pp)  81.7 us
    pmax x1, blocking collectives, shards(): step_size = 1.0 / lax.pmax(local_max, 'dp')  44.1 us
    unnamed x39, local copies, waits for them, and re-layouts  15.2 us
    while x60, local copies, waits for them, and re-layouts  7.65 us
    ppermute x4, starting transfers between devices, column_test(): even = even + ppermute(even, net_axis, pp)  6.59 us
    dot_general x2, matrix products, shards(): jnp.dot(left_cols, lax.all_gather(resid0, 'dp', axis=0, tiled=True), pref...  5.03 us
  transfers between devices with their start and end apart: 7, of which 6 were waited for; matrix products, arithmetic and copies ran while one was open for 13% of the time, Pallas kernels for 0%

profile of v1, /device:TPU:0, one launch (start us, length us, event | category | flops | bytes accessed | tf_op | source)
XLA Modules:
  0.0 204.3 jit_solution(304830258781279002)
XLA Ops:
  7.2 1.3 fusion.56
  9.1 44.1 %pmax.7 = f32[]{:T(128)} all-reduce(f32[]{:T(128)} %reduce_max.18), channel_id=1, replica_groups=mesh['section'=2,'dp'=16] {'dp'}, use_global_device_ids=true, to_apply=%region_4.5 | all-reduce | flops 1 | bytes 8 | tf_op jit(solution)/shard_map/pmax | solution.py:141
  53.9 2.0 fusion.129
  56.5 0.9 copy.18
  60.8 2.1 %reshape.70 = bf16[1728,512]{1,0:T(8,128)(2,1)} reshape(bf16[27,64,2,2,128]{4,3,2,1,0:T(2,128)(2,1)S(1)} %fusion.115) | data formatting | bytes 3538944 | tf_op jit(solution)/shard_map/reshape | solution.py:45
  62.9 0.7 broadcast.40
  63.6 22.4 %while.20 = (s32[]{:T(128)}, bf16[64,2,2,128]{3,2,1,0:T(2,128)(2,1)S(1)}, bf16[1,64,2,2,128]{4,3,2,1,0:T(2,128)(2,1)}, bf16[1,64,2,2,128]{4,3,2,1,0:T(2,128)(2,1...) while((s32[]{:T(128)}, ...), condition=%wide.region_1.2_spmd.clone, body=%wide.region_0.1_spmd.clone.sunk | while | flops 113475592 | bytes 10772739 | solution.py:119
  63.6 1.3 collective-permute-start
  64.9 1.8 collective-permute-done
  66.7 1.7 fusion.174
  71.7 0.7 reshape.79
  72.5 1.5 fusion.201
  74.1 0.6 copy-done.4
  74.8 1.3 collective-permute-start
  76.1 1.8 collective-permute-done
  77.9 1.7 fusion.174
  82.9 0.7 reshape.79
  83.7 1.5 fusion.201
  86.0 0.9 reshape_squeeze.7
  86.9 2.1 %fusion.130 = f32[1728,64]{0,1:T(8,128)S(1)} fusion(bf16[1728,512]{1,0:T(8,128)(2,1)} %reshape.70, bf16[64,512]{1,0:T(8,128)(2,1)S(1)} %reshape_squeeze.7), kind=kOutput, calls=%fused_computation.204 | convolution fusion | flops 113246208 | bytes 2277376 | tf_op jit(solution)/shard_map/dot_general | solution.py:59
  89.1 14.0 %collective-permute-done.1 = f32[1728,64]{0,1:T(8,128)S(1)} collective-permute-done((f32[1728,64]{0,1:T(8,128)S(1)}, f32[1728,64]{0,1:T(8,128)S(1)}, u32[]{:S(2)}, u32[]{:S(2)}) %collective-permute-start.1) | collective-permute-done | bytes 442400 | tf_op jit(solution)/shard_map/ppermute | solution.py:131
  103.1 1.5 collective-permute-start.2
  104.6 10.8 %collective-permute-done.2 = f32[1728,64]{0,1:T(8,128)S(1)} collective-permute-done((f32[1728,64]{0,1:T(8,128)S(1)}, f32[1728,64]{0,1:T(8,128)S(1)}, u32[]{:S(2)}, u32[]{:S(2)}) %collective-permute-start.2) | collective-permute-done | bytes 442400 | tf_op jit(solution)/shard_map/ppermute | solution.py:131
  115.5 1.6 collective-permute-start.3
  118.5 34.3 %collective-permute-done.3 = f32[1728,64]{0,1:T(8,128)S(1)} collective-permute-done((f32[1728,64]{0,1:T(8,128)S(1)}, f32[1728,64]{0,1:T(8,128)S(1)}, u32[]{:S(2)}, u32[]{:S(2)}) %collective-permute-start.3) | collective-permute-done | bytes 442400 | tf_op jit(solution)/shard_map/ppermute | solution.py:131
  152.9 3.4 %collective-permute-start.4 = (f32[1728,64]{0,1:T(8,128)S(1)}, f32[1728,64]{0,1:T(8,128)S(1)}, u32[]{:S(2)}, u32[]{:S(2)}) collective-permute-start(f32[1728,64]{0,1:T(8,128)S(1)} %add.78), channel_id=1, source_target_pairs={{0,8},{1,9},{2,10},{3,11},{4,12},{5,13},{6,14},{7,15},{8,0},{9,1},... | collective-permute-start | bytes 1327112 | tf_op jit(solution)/shard_map/ppermute | solution.py:131
  156.6 22.6 %collective-permute-done.4 = f32[1728,64]{0,1:T(8,128)S(1)} collective-permute-done((f32[1728,64]{0,1:T(8,128)S(1)}, f32[1728,64]{0,1:T(8,128)S(1)}, u32[]{:S(2)}, u32[]{:S(2)}) %collective-permute-start.4) | collective-permute-done | bytes 442400 | tf_op jit(solution)/shard_map/ppermute | solution.py:131
  179.8 8.8 %reshape.72 = bf16[1728,1728]{1,0:T(8,128)(2,1)} reshape(bf16[16,108,1728]{2,1,0:T(8,128)(2,1)} %all-gather.3.cloned.1.call-done) | data formatting | bytes 11943936
  188.6 4.0 %convolution_convert_fusion.1 = bf16[108,1728]{1,0:T(8,128)(2,1)S(1)} fusion(bf16[1728,1728]{1,0:T(8,128)(2,1)} %reshape.72, bf16[1,108,1728]{2,1,0:T(8,128)(2,1)S(1)} %copy-done.2, f32[]{:T(128)S(6)} %div.12, s32[108]{0:T(128)S(1)} %iota_add_fusion), kind=kOutput, calls=%fused_computation.115 | convolution fusion | flops 646278912 | bytes 6718900 | tf_op jit(solution)/shard_map/dot_general | solution.py:145
  193.1 1.1 fusion.54
  194.2 1.6 convolution_bitcast_fusion
  195.8 1.7 copy.17
  (121 shorter events, 14.5 us)
Async XLA Ops:
  7.2 48.8 %copy-start.5 = (bf16[1,64,1728]{2,1,0:T(8,128)(2,1)S(1)}, bf16[1,64,1728]{2,1,0:T(8,128)(2,1)}, u32[]{:S(2)}) copy-start(bf16[1,64,1728]{2,1,0:T(8,128)(2,1)} %param.11) | copy-start | bytes 663556
  7.2 50.2 %copy-start.1 = (bf16[1,1,1,64,2,2,128]{6,5,4,3,2,1,0:T(2,128)(2,1)S(1)}, bf16[1,1,1,64,2,2,128]{6,5,4,3,2,1,0:T(2,128)(2,1)}, u32[]{:S(2)}) copy-start(bf16[1,1,1,64,2,2,128]{6,5,4,3,2,1,0:T(2,128)(2,1)} %param.8) | copy-start | bytes 196612
  7.2 172.6 %all-gather.3.cloned.1.call-start = ((), (), s32[]{:S(2)}) async-start(), calls=%async_computation | async-start | bytes 6823936 | tf_op jit(solution)/shard_map/all_gather | solution.py:147
  63.6 3.1 %collective-permute-start = (bf16[64,2,2,128]{3,2,1,0:T(2,128)(2,1)S(1)}, bf16[64,2,2,128]{3,2,1,0:T(2,128)(2,1)S(1)}, u32[]{:S(2)}, u32[]{:S(2)}) collective-permute-start(bf16[64,2,2,128]{3,2,1,0:T(2,128)(2,1)S(1)} %get-tuple-element.362), channel_id=1, source_target_pairs={{16,0},{17,1},{18,2},{19,3},{20,4},{21,5},{22,6},{23,7},{24,8},{25... | collective-permute-start | bytes 196616 | tf_op jit(solution)/shard_map/while/body/eval_jaxpr/ppermute | solution.py:14
  72.4 1.6 copy-start.3
  74.1 0.6 copy-start.4
  74.8 3.1 %collective-permute-start = (bf16[64,2,2,128]{3,2,1,0:T(2,128)(2,1)S(1)}, bf16[64,2,2,128]{3,2,1,0:T(2,128)(2,1)S(1)}, u32[]{:S(2)}, u32[]{:S(2)}) collective-permute-start(bf16[64,2,2,128]{3,2,1,0:T(2,128)(2,1)S(1)} %get-tuple-element.362), channel_id=1, source_target_pairs={{16,0},{17,1},{18,2},{19,3},{20,4},{21,5},{22,6},{23,7},{24,8},{25... | collective-permute-start | bytes 196616 | tf_op jit(solution)/shard_map/while/body/eval_jaxpr/ppermute | solution.py:14
  83.7 1.6 copy-start.3
  85.3 0.6 copy-start.4
  89.0 28.1 %copy-start.6 = (bf16[1,64,64]{2,1,0:T(8,128)(2,1)S(1)}, bf16[1,64,64]{2,1,0:T(8,128)(2,1)}, u32[]{:S(2)}) copy-start(bf16[1,64,64]{2,1,0:T(8,128)(2,1)} %param.13) | copy-start | bytes 24580
  89.0 14.1 %collective-permute-start.1 = (f32[1728,64]{0,1:T(8,128)S(1)}, f32[1728,64]{0,1:T(8,128)S(1)}, u32[]{:S(2)}, u32[]{:S(2)}) collective-permute-start(f32[1728,64]{0,1:T(8,128)S(1)} %fusion.130), channel_id=1, source_target_pairs={{0,1},{1,0},{2,3},{3,2},{4,5},{5,4},{6,7},{7,6},{8,9},{9,8},{10,11... | collective-permute-start | bytes 1327112 | tf_op jit(solution)/shard_map/ppermute | solution.py:131
  103.1 12.4 %collective-permute-start.2 = (f32[1728,64]{0,1:T(8,128)S(1)}, f32[1728,64]{0,1:T(8,128)S(1)}, u32[]{:S(2)}, u32[]{:S(2)}) collective-permute-start(f32[1728,64]{0,1:T(8,128)S(1)} %add.76), channel_id=1, source_target_pairs={{0,2},{1,3},{2,0},{3,1},{4,6},{5,7},{6,4},{7,5},{8,10},{9,11},{10,... | collective-permute-start | bytes 1327112 | tf_op jit(solution)/shard_map/ppermute | solution.py:131
  115.5 37.3 %collective-permute-start.3 = (f32[1728,64]{0,1:T(8,128)S(1)}, f32[1728,64]{0,1:T(8,128)S(1)}, u32[]{:S(2)}, u32[]{:S(2)}) collective-permute-start(f32[1728,64]{0,1:T(8,128)S(1)} %add.77), channel_id=1, source_target_pairs={{0,4},{1,5},{2,6},{3,7},{4,0},{5,1},{6,2},{7,3},{8,12},{9,13},{10,... | collective-permute-start | bytes 1327112 | tf_op jit(solution)/shard_map/ppermute | solution.py:131
  152.9 26.3 %collective-permute-start.4 = (f32[1728,64]{0,1:T(8,128)S(1)}, f32[1728,64]{0,1:T(8,128)S(1)}, u32[]{:S(2)}, u32[]{:S(2)}) collective-permute-start(f32[1728,64]{0,1:T(8,128)S(1)} %add.78), channel_id=1, source_target_pairs={{0,8},{1,9},{2,10},{3,11},{4,12},{5,13},{6,14},{7,15},{8,0},{9,1},... | collective-permute-start | bytes 1327112 | tf_op jit(solution)/shard_map/ppermute | solution.py:131
  179.7 8.8 %copy-start.2 = (bf16[1,108,1728]{2,1,0:T(8,128)(2,1)S(1)}, bf16[1,108,1728]{2,1,0:T(8,128)(2,1)}, u32[]{:S(2)}) copy-start(bf16[1,108,1728]{2,1,0:T(8,128)(2,1)} %param.12) | copy-start | bytes 1119748
  188.6 4.5 %copy-start = (bf16[1728,1728]{1,0:T(8,128)(2,1)S(1)}, bf16[1728,1728]{1,0:T(8,128)(2,1)}, u32[]{:S(2)}) copy-start(bf16[1728,1728]{1,0:T(8,128)(2,1)} %reshape.72) | copy-start | bytes 17915908
Sparse Core Ops, SparseCore 0:
  56.1 110.5 all-gather.2
